TPU v7x, 32 devices: a whole 2x2x4 slice. The times are simulated.
32 devices in a mesh: blk: 8 (over z, core), grp: 4 (over y, x).
Axes of the slice: x: 2, y: 2, z: 4, core: 2. Of those that a mesh axis runs over, the one named last changes fastest.
Arguments:
- block_values: bfloat16 [1536, 16, 64, 64], P('blk', 'grp'), may hold values from -1.5 to 1.5
- block_columns: int32 [1536, 16], P('blk', 'grp'), may hold values from 0 to 1535, as said below
- row_counts: int32 [1536], P('blk'), may hold values from 6 to 16
- prolong_blocks: bfloat16 [1536, 64, 64], P(('blk', 'grp')), may hold values from -0.75 to 0.75
- aggregates: int32 [1536], P(('blk', 'grp')), may hold values from 0 to 31, as said below
Outputs:
- coarse_blocks: float32 [32, 32, 64, 64], P('grp', 'blk')
Inputs may be any that keep to these rules, and one draw needn't show every extreme that they name: `aggregates`: the aggregate of a fine block row of panel p, rows p * 192 to (p + 1) * 192 - 1, lies in p * 4 to (p + 1) * 4 - 1. `block_columns`: A block column of a row of panel p lies in a panel p + d modulo the number of panels, for some d of -2 to 2; slot 0 of each row holds the row itself.
All inputs are finite; a program needn't handle non-finite values.
Results may differ from a plain program's by a relative error of at most 0.0029.
Values may be sent and summed in bfloat16 or wider, within the bound.
No kernel may reach another device: no remote copies, remote signals or barrier semaphores. Data moves between devices by JAX's collectives and lax.ppermute only.
A program may use at most 192 MiB of HBM per device.

v0:
```python
import jax
import jax.numpy as jnp
from jax import lax
from jax.sharding import PartitionSpec as P

CB = 4


def passed_along(block, axis, distance):
    devices = range(lax.axis_size(axis))
    route = [((i - distance) % len(devices), i) for i in devices]
    return lax.ppermute(block, axis, route)


def local(block_values, block_columns, row_counts, prolong_blocks, aggregates):
    panel_length = row_counts.shape[0]
    slots_here = block_values.shape[1]
    slot_total = panel_length * slots_here
    block_size = block_values.shape[2]
    group_size = lax.axis_size("grp")
    panel_total = lax.axis_size("blk")
    coarse_count = CB * panel_total
    panel_blocks, panel_aggs = (
        lax.all_gather(prolong_blocks, "grp", axis=0, tiled=True),
        lax.all_gather(aggregates, "grp", axis=0, tiled=True),
    )
    lower = []
    upper = []
    going_down = (panel_blocks, panel_aggs)
    going_up = (panel_blocks, panel_aggs)
    for hop in range(2):
        going_down = passed_along((going_down[0], going_down[1]), "blk", 1)
        lower.insert(0, going_down)
        going_up = passed_along((going_up[0], going_up[1]), "blk", -1)
        upper.append(going_up)
    pieces = lower + [(panel_blocks, panel_aggs)] + upper
    window_blocks = jnp.concatenate([piece[0] for piece in pieces], axis=0)
    window_aggs = jnp.concatenate([piece[1] for piece in pieces], axis=0)
    own_blocks = window_blocks[2 * panel_length : 3 * panel_length]
    own_aggs = window_aggs[2 * panel_length : 3 * panel_length]
    wanted = block_columns.reshape(slot_total)
    column_panel = wanted // panel_length
    distance = jnp.mod(column_panel - lax.axis_index("blk") + 2, panel_total)
    local_rows = distance * panel_length + wanted % panel_length
    fetched = jnp.take(window_blocks, local_rows, axis=0)
    fetched_aggs = jnp.take(window_aggs, local_rows, axis=0)
    prolong_picked = fetched.reshape(panel_length, slots_here, block_size, block_size)
    product = jnp.einsum(
        "rkab,rkbc->rkac", block_values, prolong_picked, preferred_element_type=jnp.float32
    )
    slot_ids = lax.axis_index("grp") * slots_here + jnp.arange(slots_here, dtype=jnp.int32)
    live = slot_ids[None, :] < row_counts[:, None]
    product = jnp.where(live[:, :, None, None], product, 0.0).astype(jnp.bfloat16)
    restricted = jnp.einsum(
        "rba,rkbc->rkac", own_blocks, product, preferred_element_type=jnp.float32
    ).reshape(slot_total, block_size, block_size)
    local_coarse = own_aggs - lax.axis_index("blk") * CB
    target = fetched_aggs * CB + jnp.broadcast_to(
        local_coarse[:, None], (panel_length, slots_here)
    ).reshape(slot_total)
    share = coarse_count // group_size
    wanted_targets = jnp.arange(share * lax.axis_size("grp") * CB, dtype=jnp.int32)
    selector = (wanted_targets[:, None] == target[None, :]).astype(jnp.float32)
    summed = jnp.einsum(
        "ts,sab->tab",
        selector,
        restricted,
        precision=lax.Precision.HIGHEST,
        preferred_element_type=jnp.float32,
    )
    return lax.psum_scatter(
        summed.reshape(share * lax.axis_size("grp"), CB, block_size, block_size),
        "grp",
        scatter_dimension=0,
        tiled=True,
    )


def solution(mesh):
    return jax.shard_map(
        local,
        mesh=mesh,
        in_specs=(
            P("blk", "grp", None, None),
            P("blk", "grp"),
            P("blk"),
            P(("blk", "grp"), None, None),
            P(("blk", "grp")),
        ),
        out_specs=P("grp", "blk", None, None),
        check_vma=False,
    )
```

profile of v0, /device:TPU:0, one launch (start us, length us, event | category | flops | bytes accessed | tf_op | source)
XLA Modules:
  0.0 358.8 jit_solution(9059910426823162043)
XLA Ops:
  6.5 0.0 all-gather.2.cloned.1.call-start
  6.5 0.7 all-gather.2.cloned.1.call-update
  7.3 0.0 reduce-scatter.2.cloned.1.call-start
  7.3 48.5 %all-gather.2.cloned.1.call-done = bf16[192,64,64]{2,1,0:T(8,128)(2,1)} async-done(((bf16[48,64,64]{2,1,0:T(8,128)(2,1)}), bf16[192,64,64]{2,1,0:T(8,128)(2,1)}) %all-gather.2.cloned.1.call-update) | async-done | bytes 1572880 | tf_op jit(solution)/shard_map/all_gather | solution.py:24
  55.8 4.2 %copy.25 = bf16[192,64,64]{0,2,1:T(8,128)(2,1)S(1)} copy(bf16[192,64,64]{2,1,0:T(8,128)(2,1)} %all-gather.2.cloned.1.call-done) | data formatting | bytes 3145728 | tf_op jit(solution)/shard_map/all_gather | solution.py:24
  60.0 0.1 collective-permute-start.4
  60.1 3.5 collective-permute-start.6
  63.6 1.2 dynamic-slice
  65.5 0.9 dynamic-update-slice
  66.4 7.3 %all-reduce = s32[192]{0:T(256)S(1)} all-reduce(s32[192]{0:T(256)S(1)} %dynamic-update-slice), channel_id=1, replica_groups=mesh['blk'=8,'grp'=4] {'grp'}, use_global_device_ids=true, to_apply=%add | all-reduce | flops 192 | bytes 1536
  73.7 0.0 collective-permute-start
  73.7 3.5 collective-permute-start.2
  77.2 30.8 %collective-permute-done.4 = bf16[192,64,64]{0,2,1:T(8,128)(2,1)} collective-permute-done((bf16[192,64,64]{0,2,1:T(8,128)(2,1)S(1)}, bf16[192,64,64]{0,2,1:T(8,128)(2,1)}, u32[]{:S(2)}, u32[]{:S(2)}) %collective-permute-start.4) | collective-permute-done | bytes 1572896 | tf_op jit(solution)/shard_map/ppermute | solution.py:12
  108.1 0.0 collective-permute-start.5
  108.1 0.7 compare_and_fusion
  108.8 0.7 broadcast_divide_fusion
  109.5 0.0 collective-permute-done.6
  109.5 3.6 %collective-permute-start.7 = (bf16[192,64,64]{0,2,1:T(8,128)(2,1)}, bf16[192,64,64]{0,2,1:T(8,128)(2,1)}, u32[]{:S(2)}, u32[]{:S(2)}) collective-permute-start(bf16[192,64,64]{0,2,1:T(8,128)(2,1)} %collective-permute-done.6), channel_id=1, source_target_pairs={{4,0},{8,4},{12,8},{16,12},{20,16},{24,20},{28,24},{0,28},{5,1},{9... | collective-permute-start | bytes 4718600 | tf_op jit(solution)/shard_map/ppermute | solution.py:12
  113.1 0.2 copy.18
  113.3 0.1 ne.125
  113.4 0.1 copy.20
  113.5 0.1 div.28
  113.6 0.1 copy.19
  113.8 0.1 rem.106
  113.9 0.8 broadcast_compare_fusion
  114.7 0.0 collective-permute-done
  114.7 0.1 collective-permute-start.1
  114.8 0.0 collective-permute-done.2
  114.8 3.5 collective-permute-start.3
  118.3 0.1 ne.121
  118.5 0.1 div.27
  118.6 0.1 rem.96
  118.7 0.1 broadcast_in_dim.40
  118.8 0.1 reshape.243
  118.9 0.2 copy.24
  119.0 17.1 %copy.32 = bf16[192,4,64,64]{3,2,1,0:T(8,128)(2,1)} copy(bf16[192,4,64,64]{0,3,2,1:T(8,128)(2,1)} %param.5) | data formatting | bytes 12582912 | tf_op args[0]
  136.1 21.3 %collective-permute-done.1 = s32[192]{0:T(256)S(1)} collective-permute-done((s32[192]{0:T(256)S(1)}, s32[192]{0:T(256)S(1)}, u32[]{:S(2)}, u32[]{:S(2)}) %collective-permute-start.1) | collective-permute-done | bytes 800 | tf_op jit(solution)/shard_map/ppermute | solution.py:12
  157.4 0.0 collective-permute-done.3
  157.4 0.1 concatenate.6
  157.5 3.2 gather_fusion
  160.7 5.3 %copy.28 = bf16[192,64,64]{2,1,0:T(8,128)(2,1)} copy(bf16[192,64,64]{0,2,1:T(8,128)(2,1)} %collective-permute-done.4) | data formatting | bytes 3145728 | tf_op jit(solution)/shard_map/ppermute | solution.py:12
  166.0 0.0 copy-start
  166.0 5.3 %copy.29 = bf16[192,64,64]{2,1,0:T(8,128)(2,1)} copy(bf16[192,64,64]{0,2,1:T(8,128)(2,1)} %collective-permute-done.6) | data formatting | bytes 3145728 | tf_op jit(solution)/shard_map/ppermute | solution.py:12
  171.3 0.0 collective-permute-done.5
  171.3 5.2 %copy.27 = bf16[192,64,64]{2,1,0:T(8,128)(2,1)} copy(bf16[192,64,64]{0,2,1:T(8,128)(2,1)} %collective-permute-done.5) | data formatting | bytes 3145728 | tf_op jit(solution)/shard_map/ppermute | solution.py:12
  176.5 0.0 copy-start.1
  176.5 4.4 %constant_dynamic-update-slice_fusion.4 = bf16[960,64,64]{2,1,0:T(8,128)(2,1)} fusion(bf16[192,64,64]{2,1,0:T(8,128)(2,1)} %copy.27), kind=kLoop, calls=%fused_computation.31 | loop fusion | bytes 4718592
  180.8 4.3 %constant_dynamic-update-slice_fusion.3 = bf16[960,64,64]{2,1,0:T(8,128)(2,1)} fusion(bf16[960,64,64]{2,1,0:T(8,128)(2,1)} %constant_dynamic-update-slice_fusion.4, bf16[192,64,64]{2,1,0:T(8,128)(2,1)} %copy.28), kind=kLoop, calls=%fused_computation.30 | loop fusion | bytes 6291456
  185.1 0.0 copy-done
  185.1 2.4 constant_dynamic-update-slice_fusion.2
  187.5 0.0 copy-done.1
  187.5 2.4 constant_dynamic-update-slice_fusion.1
  189.9 0.0 collective-permute-done.7
  189.9 5.3 %copy.30 = bf16[192,64,64]{2,1,0:T(8,128)(2,1)} copy(bf16[192,64,64]{0,2,1:T(8,128)(2,1)} %collective-permute-done.7) | data formatting | bytes 3145728 | tf_op jit(solution)/shard_map/ppermute | solution.py:12
  195.1 4.2 %constant_dynamic-update-slice_fusion = bf16[960,64,64]{2,1,0:T(8,128)(2,1)} fusion(bf16[960,64,64]{2,1,0:T(8,128)(2,1)} %constant_dynamic-update-slice_fusion.1, bf16[192,64,64]{2,1,0:T(8,128)(2,1)} %copy.30), kind=kLoop, calls=%fused_computation.27 | loop fusion | bytes 6291456 | tf_op jit(solution)/shard_map/concatenate | solution.py:37
  199.3 25.3 %gather_fusion.1 = bf16[768,64,64]{2,1,0:T(8,128)(2,1)} fusion(bf16[960,64,64]{2,1,0:T(8,128)(2,1)} %constant_dynamic-update-slice_fusion, s32[1024]{0:T(1024)S(1)} %pad_clamp_fusion), kind=kCustom, calls=%fused_computation.1 | custom fusion | bytes 12585984 | tf_op jit(solution)/shard_map/jit(_take)/gather | solution.py:45
  224.6 16.6 %copy.31 = bf16[192,4,64,64]{2,3,1,0:T(8,128)(2,1)} copy(bf16[192,4,64,64]{3,2,1,0:T(8,128)(2,1)} %bitcast.23) | data formatting | bytes 12582912 | tf_op jit(solution)/shard_map/jit(_take)/gather | solution.py:45
  241.3 22.3 %fusion.1 = f32[192,4,64,64]{3,2,1,0:T(8,128)} fusion(pred[192,4]{1,0:T(8,128)(4,1)S(1)} %broadcast_compare_fusion, bf16[192,4,64,64]{3,2,1,0:T(8,128)(2,1)} %copy.32, bf16[192,4,64,64]{2,3,1,0:T(8,128)(2,1)} %copy.31, pred[192,4]{1,0:T(8,128)(4,1)S(1)} %copy.24, bf16[192,64,64]{2,1,0:T(8,128)(2,1)S(1)} %copy-done), kind=kOutput, calls=%fused_computation.4 | convolution fusion | flops 814743552 | bytes 26740224 | tf_op jit(solution)/shard_map/rba,rkbc->rkac/dot_general | solution.py:54
  263.6 22.3 %copy.33 = f32[768,64,64]{0,2,1:T(8,128)} copy(f32[768,64,64]{1,2,0:T(8,128)} %bitcast.22) | data formatting | bytes 25165824 | tf_op jit(solution)/shard_map/reshape | solution.py:56
  285.9 13.4 %fusion.3 = f32[32,4,64,64]{3,0,2,1:T(8,128)} fusion(f32[768,64,64]{0,2,1:T(8,128)} %copy.33, s32[768]{0:T(1024)S(1)} %multiply_add_fusion, s32[32,4]{0,1:T(4,128)S(1)} %multiply_add_fusion.1), kind=kOutput, calls=%fused_computation.5 | convolution fusion | flops 4831936512 | bytes 14683648 | tf_op jit(solution)/shard_map/ts,sab->tab/dot_general | solution.py:64
  299.3 0.0 reduce-scatter.2.cloned.1.call-update
  299.3 50.2 %reduce-scatter.2.cloned.1.call-done = f32[8,4,64,64]{3,0,2,1:T(8,128)} async-done(((f32[32,4,64,64]{3,0,2,1:T(8,128)}), f32[8,4,64,64]{3,0,2,1:T(8,128)}) %reduce-scatter.2.cloned.1.call-update) | async-done | bytes 524304 | tf_op jit(solution)/shard_map/reduce_scatter | solution.py:71
  349.5 2.4 copy.34
  (7 shorter events, 0.1 us)
Async XLA Ops:
  6.5 49.2 %all-gather.2.cloned.1.call-start = ((), (), s32[]{:S(2)}) async-start(), calls=%async_computation.1 | async-start | bytes 3932160 | tf_op jit(solution)/shard_map/all_gather | solution.py:24
  7.3 342.3 %reduce-scatter.2.cloned.1.call-start = ((), (), s32[]{:S(2)}) async-start(), calls=%async_computation.2 | async-start | bytes 5242880 | tf_op jit(solution)/shard_map/reduce_scatter | solution.py:71
  60.0 48.1 %collective-permute-start.4 = (bf16[192,64,64]{0,2,1:T(8,128)(2,1)S(1)}, bf16[192,64,64]{0,2,1:T(8,128)(2,1)}, u32[]{:S(2)}, u32[]{:S(2)}) collective-permute-start(bf16[192,64,64]{0,2,1:T(8,128)(2,1)S(1)} %copy.25), channel_id=1, source_target_pairs={{28,0},{0,4},{4,8},{8,12},{12,16},{16,20},{20,24},{24,28},{29,1},{... | collective-permute-start | bytes 4718600 | tf_op jit(solution)/shard_map/ppermute | solution.py:12
  60.1 49.4 %collective-permute-start.6 = (bf16[192,64,64]{0,2,1:T(8,128)(2,1)S(1)}, bf16[192,64,64]{0,2,1:T(8,128)(2,1)}, u32[]{:S(2)}, u32[]{:S(2)}) collective-permute-start(bf16[192,64,64]{0,2,1:T(8,128)(2,1)S(1)} %copy.25), channel_id=1, source_target_pairs={{4,0},{8,4},{12,8},{16,12},{20,16},{24,20},{28,24},{0,28},{5,1},{9... | collective-permute-start | bytes 4718600 | tf_op jit(solution)/shard_map/ppermute | solution.py:12
  73.7 41.0 %collective-permute-start = (s32[192]{0:T(256)S(1)}, s32[192]{0:T(256)S(1)}, u32[]{:S(2)}, u32[]{:S(2)}) collective-permute-start(s32[192]{0:T(256)S(1)} %all-reduce), channel_id=1, source_target_pairs={{28,0},{0,4},{4,8},{8,12},{12,16},{16,20},{20,24},{24,28},{29,1},{... | collective-permute-start | bytes 2312 | tf_op jit(solution)/shard_map/ppermute | solution.py:12
  73.7 41.1 %collective-permute-start.2 = (s32[192]{0:T(256)S(1)}, s32[192]{0:T(256)S(1)}, u32[]{:S(2)}, u32[]{:S(2)}) collective-permute-start(s32[192]{0:T(256)S(1)} %all-reduce), channel_id=1, source_target_pairs={{4,0},{8,4},{12,8},{16,12},{20,16},{24,20},{28,24},{0,28},{5,1},{9... | collective-permute-start | bytes 2312 | tf_op jit(solution)/shard_map/ppermute | solution.py:12
  108.1 63.2 %collective-permute-start.5 = (bf16[192,64,64]{0,2,1:T(8,128)(2,1)}, bf16[192,64,64]{0,2,1:T(8,128)(2,1)}, u32[]{:S(2)}, u32[]{:S(2)}) collective-permute-start(bf16[192,64,64]{0,2,1:T(8,128)(2,1)} %collective-permute-done.4), channel_id=1, source_target_pairs={{28,0},{0,4},{4,8},{8,12},{12,16},{16,20},{20,24},{24,28},{29,1},{... | collective-permute-start | bytes 4718600 | tf_op jit(solution)/shard_map/ppermute | solution.py:12
  109.5 80.4 %collective-permute-start.7 = (bf16[192,64,64]{0,2,1:T(8,128)(2,1)}, bf16[192,64,64]{0,2,1:T(8,128)(2,1)}, u32[]{:S(2)}, u32[]{:S(2)}) collective-permute-start(bf16[192,64,64]{0,2,1:T(8,128)(2,1)} %collective-permute-done.6), channel_id=1, source_target_pairs={{4,0},{8,4},{12,8},{16,12},{20,16},{24,20},{28,24},{0,28},{5,1},{9... | collective-permute-start | bytes 4718600 | tf_op jit(solution)/shard_map/ppermute | solution.py:12
  114.7 42.7 %collective-permute-start.1 = (s32[192]{0:T(256)S(1)}, s32[192]{0:T(256)S(1)}, u32[]{:S(2)}, u32[]{:S(2)}) collective-permute-start(s32[192]{0:T(256)S(1)} %collective-permute-done), channel_id=1, source_target_pairs={{28,0},{0,4},{4,8},{8,12},{12,16},{16,20},{20,24},{24,28},{29,1},{... | collective-permute-start | bytes 2312 | tf_op jit(solution)/shard_map/ppermute | solution.py:12
  114.8 42.6 %collective-permute-start.3 = (s32[192]{0:T(256)S(1)}, s32[192]{0:T(256)S(1)}, u32[]{:S(2)}, u32[]{:S(2)}) collective-permute-start(s32[192]{0:T(256)S(1)} %collective-permute-done.2), channel_id=1, source_target_pairs={{4,0},{8,4},{12,8},{16,12},{20,16},{24,20},{28,24},{0,28},{5,1},{9... | collective-permute-start | bytes 2312 | tf_op jit(solution)/shard_map/ppermute | solution.py:12
  166.0 19.1 %copy-start = (bf16[192,64,64]{2,1,0:T(8,128)(2,1)S(1)}, bf16[192,64,64]{2,1,0:T(8,128)(2,1)}, u32[]{:S(2)}) copy-start(bf16[192,64,64]{2,1,0:T(8,128)(2,1)} %all-gather.2.cloned.1.call-done) | copy-start | bytes 4718596
  176.5 11.0 %copy-start.1 = (bf16[192,64,64]{2,1,0:T(8,128)(2,1)S(1)}, bf16[192,64,64]{2,1,0:T(8,128)(2,1)}, u32[]{:S(2)}) copy-start(bf16[192,64,64]{2,1,0:T(8,128)(2,1)} %copy.29) | copy-start | bytes 4718596
Sparse Core Ops, SparseCore 0:
  9.2 46.5 all-gather.1
  299.5 50.0 reduce-scatter.1
where the time goes:
time: 361 us; the launch traced here: 359 us
  waiting for transfers between devices  152 us (42%)
  local copies, waits for them, and re-layouts  133 us (37%)
  matrix products  35.7 us (10%)
  starting transfers between devices  14.3 us (4%)
  between operations  14.2 us (4%)
  blocking collectives  7.32 us (2%)
    ppermute x8, waiting for transfers between devices, passed_along(): return lax.ppermute(block, axis, route)  52.2 us
    reduce_scatter x1, waiting for transfers between devices, local(): lax.psum_scatter(summed.reshape(share * lax.axis_size('grp'), CB, block_s...  50.2 us
    all_gather x1, waiting for transfers between devices, local(): lax.all_gather(prolong_blocks, 'grp', axis=0, tiled=True)  48.5 us
    gather x2, local copies, waits for them, and re-layouts, local(): fetched = jnp.take(window_blocks, local_rows, axis=0)  41.9 us
    unnamed x12, local copies, waits for them, and re-layouts  32.5 us
    dot_general x1, matrix products, local(): jnp.einsum('rba,rkbc->rkac', own_blocks, product, preferred_element_type=...  22.3 us
    reshape x1, local copies, waits for them, and re-layouts, local(): restricted = jnp.einsum('rba,rkbc->rkac', own_blocks, product, preferred_...  22.3 us
    ppermute x4, local copies, waits for them, and re-layouts, passed_along(): return lax.ppermute(block, axis, route)  21 us
  transfers between devices with their start and end apart: 10, of which 4 were waited for; matrix products, arithmetic and copies ran while one was open for 15% of the time, Pallas kernels for 0%

commit v1 on v0

--- a/solution.py
+++ b/solution.py
@@ -1,9 +1,36 @@
+import functools
 import jax
 import jax.numpy as jnp
 from jax import lax
 from jax.sharding import PartitionSpec as P
 
 CB = 4
+
+
+def tokens_wrap(x_part, d0):
+    z1, block_now, t_next = (jax.lax.axis_size("grp"), jax.lax.axis_index("grp"), x_part.shape[d0])
+    t1 = met_up = x_part
+    z2 = lax.dynamic_update_slice_in_dim(
+        jnp.zeros(
+            [hop_no * z1 if it == d0 else hop_no for it, hop_no in enumerate(x_part.shape)],
+            x_part.dtype,
+        ),
+        x_part,
+        block_now * t_next,
+        axis=d0,
+    )
+    for pp in range(1, z1 // 2 + 1):
+        t1 = jax.lax.ppermute(t1, "grp", [(it, (it + 1) % z1) for it in range(z1)])
+        z2 = lax.dynamic_update_slice_in_dim(z2, t1, (block_now - pp) % z1 * t_next, axis=d0)
+        if 2 * pp < z1:
+            met_up = jax.lax.ppermute(met_up, "grp", [(it, (it - 1) % z1) for it in range(z1)])
+            z2 = lax.dynamic_update_slice_in_dim(
+                z2, met_up, (block_now + pp) % z1 * t_next, axis=d0
+            )
+    return z2
+
+
+use_loops_in = functools.partial(tokens_wrap, d0=0)
 
 
 def passed_along(block, axis, distance):
@@ -21,7 +48,7 @@
     panel_total = lax.axis_size("blk")
     coarse_count = CB * panel_total
     panel_blocks, panel_aggs = (
-        lax.all_gather(prolong_blocks, "grp", axis=0, tiled=True),
+        use_loops_in(prolong_blocks),
         lax.all_gather(aggregates, "grp", axis=0, tiled=True),
     )
     lower = []

time: 361 us -> 352 us (0.975)
  local copies, waits for them, and re-layouts: 133 us -> 120 us
  waiting for transfers between devices: 152 us -> 159 us
    all_gather x1 -> x0, waiting for transfers between devices: 48.5 us -> none  [local(): lax.all_gather(prolong_blocks, 'grp', axis=0, tiled=True)]
    ppermute x0 -> x3, waiting for transfers between devices: none -> 45.8 us  [the longest x2 32.8 us: tokens_wrap(): t1 = jax.lax.ppermute(t1, 'grp', [(it, (it + 1) % z1) for it in range(z1)])]
    gather x2 -> x1, local copies, waits for them, and re-layouts: 41.9 us -> 25.3 us  [local(): fetched = jnp.take(window_blocks, local_rows, axis=0)]
    dynamic_update_slice x0 -> x5, local copies, waits for them, and re-layouts: none -> 7.65 us  [the longest x3 5.17 us: tokens_wrap(): lax.dynamic_update_slice_in_dim(z2, t1, (block_now - pp) % z1 * t_next, a...]
    ppermute x8, waiting for transfers between devices: 52.2 us -> 58.5 us  [passed_along(): return lax.ppermute(block, axis, route)]
    ppermute x8, starting transfers between devices: 14.3 us -> 8.58 us  [passed_along(): return lax.ppermute(block, axis, route)]
    ppermute x0 -> x3, starting transfers between devices: none -> 5.1 us  [the longest x2 4.08 us: tokens_wrap(): t1 = jax.lax.ppermute(t1, 'grp', [(it, (it + 1) % z1) for it in range(z1)])]
    reduce_scatter x1, waiting for transfers between devices: 50.2 us -> 54.9 us  [local(): lax.psum_scatter(summed.reshape(share * lax.axis_size('grp'), CB, block_s...]
  transfers between devices with their start and end apart: 10 -> 12, of which waited for: 4 -> 7; matrix products, arithmetic and copies ran while one was open for 15% -> 16% of each run, Pallas kernels for 0% -> 0%
where the time goes in v1:
time: 352 us; the launch traced here: 351 us
  waiting for transfers between devices  159 us (45%)
  local copies, waits for them, and re-layouts  120 us (34%)
  matrix products  36.3 us (10%)
  between operations  14.2 us (4%)
  starting transfers between devices  13.7 us (4%)
  blocking collectives  7.56 us (2%)
    ppermute x8, waiting for transfers between devices, passed_along(): return lax.ppermute(block, axis, route)  58.5 us
    reduce_scatter x1, waiting for transfers between devices, local(): lax.psum_scatter(summed.reshape(share * lax.axis_size('grp'), CB, block_s...  54.9 us
    ppermute x2, waiting for transfers between devices, tokens_wrap(): t1 = jax.lax.ppermute(t1, 'grp', [(it, (it + 1) % z1) for it in range(z1)])  32.8 us
    unnamed x18, local copies, waits for them, and re-layouts  31.2 us
    gather x1, local copies, waits for them, and re-layouts, local(): fetched = jnp.take(window_blocks, local_rows, axis=0)  25.3 us
    dot_general x1, matrix products, local(): jnp.einsum('rba,rkbc->rkac', own_blocks, product, preferred_element_type=...  22.9 us
    reshape x1, local copies, waits for them, and re-layouts, local(): restricted = jnp.einsum('rba,rkbc->rkac', own_blocks, product, preferred_...  22.4 us
    ppermute x4, local copies, waits for them, and re-layouts, passed_along(): return lax.ppermute(block, axis, route)  20.9 us
  transfers between devices with their start and end apart: 12, of which 7 were waited for; matrix products, arithmetic and copies ran while one was open for 16% of the time, Pallas kernels for 0%

profile of v1, /device:TPU:0, one launch (start us, length us, event | category | flops | bytes accessed | tf_op | source)
XLA Modules:
  0.0 350.9 jit_solution(5824317539116562510)
XLA Ops:
  6.5 0.0 reduce-scatter.2.cloned.1.call-start
  6.6 3.0 collective-permute-start.4
  9.6 1.0 collective-permute-start.5
  10.6 18.6 %collective-permute-done.4 = bf16[48,64,64]{2,1,0:T(8,128)(2,1)} collective-permute-done((bf16[48,64,64]{2,1,0:T(8,128)(2,1)}, bf16[48,64,64]{2,1,0:T(8,128)(2,1)}, u32[]{:S(2)}, u32[]{:S(2)}) %collective-permute-start.4) | collective-permute-done | bytes 393248 | tf_op jit(solution)/shard_map/ppermute | solution.py:23
  29.3 1.1 collective-permute-start.6
  30.3 0.8 broadcast_in_dim.46
  31.1 1.2 constant_dynamic-update-slice_fusion.8
  32.4 1.2 constant_dynamic-update-slice_fusion.7
  33.6 13.0 %collective-permute-done.5 = bf16[48,64,64]{2,1,0:T(8,128)(2,1)} collective-permute-done((bf16[48,64,64]{2,1,0:T(8,128)(2,1)}, bf16[48,64,64]{2,1,0:T(8,128)(2,1)}, u32[]{:S(2)}, u32[]{:S(2)}) %collective-permute-start.5) | collective-permute-done | bytes 393248 | tf_op jit(solution)/shard_map/ppermute | solution.py:26
  46.6 1.2 constant_dynamic-update-slice_fusion.6
  47.9 14.1 %collective-permute-done.6 = bf16[48,64,64]{2,1,0:T(8,128)(2,1)S(1)} collective-permute-done((bf16[48,64,64]{2,1,0:T(8,128)(2,1)}, bf16[48,64,64]{2,1,0:T(8,128)(2,1)S(1)}, u32[]{:S(2)}, u32[]{:S(2)}) %collective-permute-start.6) | collective-permute-done | bytes 393248 | tf_op jit(solution)/shard_map/ppermute | solution.py:23
  62.0 0.1 constant_dynamic-update-slice_fusion.5
  62.1 3.8 %copy.40 = bf16[192,64,64]{0,2,1:T(8,128)(2,1)} copy(bf16[192,64,64]{2,1,0:T(8,128)(2,1)S(1)} %constant_dynamic-update-slice_fusion.5) | data formatting | bytes 3145728 | tf_op jit(solution)/shard_map/dynamic_update_slice | solution.py:24
  66.0 0.0 collective-permute-start.7
  66.0 3.5 %collective-permute-start.9 = (bf16[192,64,64]{0,2,1:T(8,128)(2,1)}, bf16[192,64,64]{0,2,1:T(8,128)(2,1)}, u32[]{:S(2)}, u32[]{:S(2)}) collective-permute-start(bf16[192,64,64]{0,2,1:T(8,128)(2,1)} %copy.40), channel_id=1, source_target_pairs={{4,0},{8,4},{12,8},{16,12},{20,16},{24,20},{28,24},{0,28},{5,1},{9... | collective-permute-start | bytes 4718600 | tf_op jit(solution)/shard_map/ppermute | solution.py:39
  69.5 0.6 dynamic-slice
  70.8 0.2 dynamic-update-slice
  71.0 7.6 %all-reduce = s32[192]{0:T(256)S(1)} all-reduce(s32[192]{0:T(256)S(1)} %dynamic-update-slice), channel_id=1, replica_groups=mesh['blk'=8,'grp'=4] {'grp'}, use_global_device_ids=true, to_apply=%add | all-reduce | flops 192 | bytes 1536
  78.6 0.0 collective-permute-start.2
  78.6 0.5 collective-permute-start
  79.1 34.6 %collective-permute-done.7 = bf16[192,64,64]{0,2,1:T(8,128)(2,1)} collective-permute-done((bf16[192,64,64]{0,2,1:T(8,128)(2,1)}, bf16[192,64,64]{0,2,1:T(8,128)(2,1)}, u32[]{:S(2)}, u32[]{:S(2)}) %collective-permute-start.7) | collective-permute-done | bytes 1572896 | tf_op jit(solution)/shard_map/ppermute | solution.py:39
  113.7 0.0 collective-permute-start.8
  113.8 0.0 collective-permute-done.9
  113.8 3.6 %collective-permute-start.10 = (bf16[192,64,64]{0,2,1:T(8,128)(2,1)}, bf16[192,64,64]{0,2,1:T(8,128)(2,1)}, u32[]{:S(2)}, u32[]{:S(2)}) collective-permute-start(bf16[192,64,64]{0,2,1:T(8,128)(2,1)} %collective-permute-done.9), channel_id=1, source_target_pairs={{4,0},{8,4},{12,8},{16,12},{20,16},{24,20},{28,24},{0,28},{5,1},{9... | collective-permute-start | bytes 4718600 | tf_op jit(solution)/shard_map/ppermute | solution.py:39
  117.4 0.2 copy.33
  117.5 0.1 ne.139
  117.7 0.1 copy.35
  117.8 0.1 div.28
  117.9 0.1 copy.34
  118.0 0.1 rem.146
  118.2 0.1 broadcast_compare_fusion
  118.3 0.0 collective-permute-done.2
  118.3 0.9 collective-permute-start.3
  119.3 0.0 collective-permute-done
  119.3 0.0 collective-permute-start.1
  119.3 0.1 ne.135
  119.4 0.1 div.27
  119.5 0.1 rem.136
  119.6 0.2 copy.39
  119.8 0.1 broadcast_in_dim.43
  119.9 0.1 reshape.243
  120.0 17.1 %copy.47 = bf16[192,4,64,64]{3,2,1,0:T(8,128)(2,1)} copy(bf16[192,4,64,64]{0,3,2,1:T(8,128)(2,1)} %param.5) | data formatting | bytes 12582912 | tf_op args[0]
  137.0 22.4 %collective-permute-done.3 = s32[192]{0:T(256)S(1)} collective-permute-done((s32[192]{0:T(256)S(1)}, s32[192]{0:T(256)S(1)}, u32[]{:S(2)}, u32[]{:S(2)}) %collective-permute-start.3) | collective-permute-done | bytes 800 | tf_op jit(solution)/shard_map/ppermute | solution.py:39
  159.4 1.5 collective-permute-done.1
  160.9 0.1 concatenate.6
  161.0 3.2 gather_fusion
  164.2 5.2 %copy.43 = bf16[192,64,64]{2,1,0:T(8,128)(2,1)} copy(bf16[192,64,64]{0,2,1:T(8,128)(2,1)} %collective-permute-done.7) | data formatting | bytes 3145728 | tf_op jit(solution)/shard_map/ppermute | solution.py:39
  169.4 5.3 %copy.44 = bf16[192,64,64]{2,1,0:T(8,128)(2,1)} copy(bf16[192,64,64]{0,2,1:T(8,128)(2,1)} %collective-permute-done.9) | data formatting | bytes 3145728 | tf_op jit(solution)/shard_map/ppermute | solution.py:39
  174.6 0.0 collective-permute-done.8
  174.6 5.3 %copy.42 = bf16[192,64,64]{2,1,0:T(8,128)(2,1)} copy(bf16[192,64,64]{0,2,1:T(8,128)(2,1)} %collective-permute-done.8) | data formatting | bytes 3145728 | tf_op jit(solution)/shard_map/ppermute | solution.py:39
  179.9 4.4 %constant_dynamic-update-slice_fusion.4 = bf16[960,64,64]{2,1,0:T(8,128)(2,1)} fusion(bf16[192,64,64]{2,1,0:T(8,128)(2,1)} %copy.42), kind=kLoop, calls=%fused_computation.31 | loop fusion | bytes 4718592
  184.3 4.2 %constant_dynamic-update-slice_fusion.3 = bf16[960,64,64]{2,1,0:T(8,128)(2,1)} fusion(bf16[960,64,64]{2,1,0:T(8,128)(2,1)} %constant_dynamic-update-slice_fusion.4, bf16[192,64,64]{2,1,0:T(8,128)(2,1)} %copy.43), kind=kLoop, calls=%fused_computation.30 | loop fusion | bytes 6291456
  188.5 2.4 constant_dynamic-update-slice_fusion.2
  190.9 2.3 constant_dynamic-update-slice_fusion.1
  193.3 0.0 collective-permute-done.10
  193.3 5.3 %copy.45 = bf16[192,64,64]{2,1,0:T(8,128)(2,1)} copy(bf16[192,64,64]{0,2,1:T(8,128)(2,1)} %collective-permute-done.10) | data formatting | bytes 3145728 | tf_op jit(solution)/shard_map/ppermute | solution.py:39
  198.5 4.2 %constant_dynamic-update-slice_fusion = bf16[960,64,64]{2,1,0:T(8,128)(2,1)} fusion(bf16[960,64,64]{2,1,0:T(8,128)(2,1)} %constant_dynamic-update-slice_fusion.1, bf16[192,64,64]{2,1,0:T(8,128)(2,1)} %copy.45), kind=kLoop, calls=%fused_computation.27 | loop fusion | bytes 6291456 | tf_op jit(solution)/shard_map/concatenate | solution.py:64
  202.7 25.3 %gather_fusion.1 = bf16[768,64,64]{2,1,0:T(8,128)(2,1)} fusion(bf16[960,64,64]{2,1,0:T(8,128)(2,1)} %constant_dynamic-update-slice_fusion, s32[1024]{0:T(1024)S(1)} %pad_clamp_fusion), kind=kCustom, calls=%fused_computation.1 | custom fusion | bytes 12585984 | tf_op jit(solution)/shard_map/jit(_take)/gather | solution.py:72
  228.0 22.9 %fusion.1 = f32[192,4,64,64]{3,2,1,0:T(8,128)} fusion(pred[192,4]{1,0:T(8,128)(4,1)S(1)} %broadcast_compare_fusion, bf16[192,4,64,64]{3,2,1,0:T(8,128)(2,1)} %copy.47, bf16[192,4,64,64]{3,2,1,0:T(8,128)(2,1)} %bitcast.23, pred[192,4]{1,0:T(8,128)(4,1)S(1)} %copy.39, bf16[192,64,64]{2,1,0:T(8,128)(2,1)S(1)} %constant_dynamic-update-slice_fusion.5), kind=kOutput, calls=%fused_computation.4 | convolution fusion | flops 814743552 | bytes 26740224 | tf_op jit(solution)/shard_map/rba,rkbc->rkac/dot_general | solution.py:81
  251.0 22.4 %copy.48 = f32[768,64,64]{0,2,1:T(8,128)} copy(f32[768,64,64]{1,2,0:T(8,128)} %bitcast.22) | data formatting | bytes 25165824 | tf_op jit(solution)/shard_map/reshape | solution.py:83
  273.3 13.4 %fusion.3 = f32[32,4,64,64]{3,0,2,1:T(8,128)} fusion(f32[768,64,64]{0,2,1:T(8,128)} %copy.48, s32[768]{0:T(1024)S(1)} %multiply_add_fusion, s32[32,4]{0,1:T(4,128)S(1)} %multiply_add_fusion.1), kind=kOutput, calls=%fused_computation.5 | convolution fusion | flops 4831936512 | bytes 14683648 | tf_op jit(solution)/shard_map/ts,sab->tab/dot_general | solution.py:91
  286.8 0.0 reduce-scatter.2.cloned.1.call-update
  286.8 54.9 %reduce-scatter.2.cloned.1.call-done = f32[8,4,64,64]{3,0,2,1:T(8,128)} async-done(((f32[32,4,64,64]{3,0,2,1:T(8,128)}), f32[8,4,64,64]{3,0,2,1:T(8,128)}) %reduce-scatter.2.cloned.1.call-update) | async-done | bytes 524304 | tf_op jit(solution)/shard_map/reduce_scatter | solution.py:98
  341.6 2.4 copy.49
  (19 shorter events, 0.1 us)
Async XLA Ops:
  6.5 63.0 %copy-start.4 = (u32[32]{0:T(128)S(1)}, u32[32]{0:T(128)}, u32[]{:S(2)}) copy-start(u32[32]{0:T(128)} %constant.113) | copy-start | bytes 388
  6.5 64.2 %copy-start.3 = (s32[48]{0:T(128)S(1)}, s32[48]{0:T(128)}, u32[]{:S(2)}) copy-start(s32[48]{0:T(128)} %param.9) | copy-start | bytes 580
  6.5 107.2 %copy-start.1 = (s32[192,4]{0,1:T(4,128)S(1)}, s32[192,4]{0,1:T(4,128)}, u32[]{:S(2)}) copy-start(s32[192,4]{0,1:T(4,128)} %param.6) | copy-start | bytes 9220
  6.5 111.7 %copy-start.2 = (s32[192]{0:T(256)S(1)}, s32[192]{0:T(256)}, u32[]{:S(2)}) copy-start(s32[192]{0:T(256)} %param.7) | copy-start | bytes 2308
  6.5 335.1 %reduce-scatter.2.cloned.1.call-start = ((), (), s32[]{:S(2)}) async-start(), calls=%async_computation.1 | async-start | bytes 5242880 | tf_op jit(solution)/shard_map/reduce_scatter | solution.py:98
  6.6 22.7 %collective-permute-start.4 = (bf16[48,64,64]{2,1,0:T(8,128)(2,1)}, bf16[48,64,64]{2,1,0:T(8,128)(2,1)}, u32[]{:S(2)}, u32[]{:S(2)}) collective-permute-start(bf16[48,64,64]{2,1,0:T(8,128)(2,1)} %param.8), channel_id=1, source_target_pairs={{0,1},{1,2},{2,3},{3,0},{4,5},{5,6},{6,7},{7,4},{8,9},{9,10},{10,1... | collective-permute-start | bytes 1179656 | tf_op jit(solution)/shard_map/ppermute | solution.py:23
  9.6 37.0 %collective-permute-start.5 = (bf16[48,64,64]{2,1,0:T(8,128)(2,1)}, bf16[48,64,64]{2,1,0:T(8,128)(2,1)}, u32[]{:S(2)}, u32[]{:S(2)}) collective-permute-start(bf16[48,64,64]{2,1,0:T(8,128)(2,1)} %param.8), channel_id=1, source_target_pairs={{0,3},{1,0},{2,1},{3,2},{4,7},{5,4},{6,5},{7,6},{8,11},{9,8},{10,9... | collective-permute-start | bytes 1179656 | tf_op jit(solution)/shard_map/ppermute | solution.py:26
  29.3 32.8 %collective-permute-start.6 = (bf16[48,64,64]{2,1,0:T(8,128)(2,1)}, bf16[48,64,64]{2,1,0:T(8,128)(2,1)S(1)}, u32[]{:S(2)}, u32[]{:S(2)}) collective-permute-start(bf16[48,64,64]{2,1,0:T(8,128)(2,1)} %collective-permute-done.4), channel_id=1, source_target_pairs={{0,1},{1,2},{2,3},{3,0},{4,5},{5,6},{6,7},{7,4},{8,9},{9,10},{10,1... | collective-permute-start | bytes 1179656 | tf_op jit(solution)/shard_map/ppermute | solution.py:23
  66.0 47.8 %collective-permute-start.7 = (bf16[192,64,64]{0,2,1:T(8,128)(2,1)}, bf16[192,64,64]{0,2,1:T(8,128)(2,1)}, u32[]{:S(2)}, u32[]{:S(2)}) collective-permute-start(bf16[192,64,64]{0,2,1:T(8,128)(2,1)} %copy.40), channel_id=1, source_target_pairs={{28,0},{0,4},{4,8},{8,12},{12,16},{16,20},{20,24},{24,28},{29,1},{... | collective-permute-start | bytes 4718600 | tf_op jit(solution)/shard_map/ppermute | solution.py:39
  66.0 47.8 %collective-permute-start.9 = (bf16[192,64,64]{0,2,1:T(8,128)(2,1)}, bf16[192,64,64]{0,2,1:T(8,128)(2,1)}, u32[]{:S(2)}, u32[]{:S(2)}) collective-permute-start(bf16[192,64,64]{0,2,1:T(8,128)(2,1)} %copy.40), channel_id=1, source_target_pairs={{4,0},{8,4},{12,8},{16,12},{20,16},{24,20},{28,24},{0,28},{5,1},{9... | collective-permute-start | bytes 4718600 | tf_op jit(solution)/shard_map/ppermute | solution.py:39
  78.6 39.8 %collective-permute-start.2 = (s32[192]{0:T(256)S(1)}, s32[192]{0:T(256)S(1)}, u32[]{:S(2)}, u32[]{:S(2)}) collective-permute-start(s32[192]{0:T(256)S(1)} %all-reduce), channel_id=1, source_target_pairs={{4,0},{8,4},{12,8},{16,12},{20,16},{24,20},{28,24},{0,28},{5,1},{9... | collective-permute-start | bytes 2312 | tf_op jit(solution)/shard_map/ppermute | solution.py:39
  78.6 40.7 %collective-permute-start = (s32[192]{0:T(256)S(1)}, s32[192]{0:T(256)S(1)}, u32[]{:S(2)}, u32[]{:S(2)}) collective-permute-start(s32[192]{0:T(256)S(1)} %all-reduce), channel_id=1, source_target_pairs={{28,0},{0,4},{4,8},{8,12},{12,16},{16,20},{20,24},{24,28},{29,1},{... | collective-permute-start | bytes 2312 | tf_op jit(solution)/shard_map/ppermute | solution.py:39
  113.7 60.9 %collective-permute-start.8 = (bf16[192,64,64]{0,2,1:T(8,128)(2,1)}, bf16[192,64,64]{0,2,1:T(8,128)(2,1)}, u32[]{:S(2)}, u32[]{:S(2)}) collective-permute-start(bf16[192,64,64]{0,2,1:T(8,128)(2,1)} %collective-permute-done.7), channel_id=1, source_target_pairs={{28,0},{0,4},{4,8},{8,12},{12,16},{16,20},{20,24},{24,28},{29,1},{... | collective-permute-start | bytes 4718600 | tf_op jit(solution)/shard_map/ppermute | solution.py:39
  113.8 79.5 %collective-permute-start.10 = (bf16[192,64,64]{0,2,1:T(8,128)(2,1)}, bf16[192,64,64]{0,2,1:T(8,128)(2,1)}, u32[]{:S(2)}, u32[]{:S(2)}) collective-permute-start(bf16[192,64,64]{0,2,1:T(8,128)(2,1)} %collective-permute-done.9), channel_id=1, source_target_pairs={{4,0},{8,4},{12,8},{16,12},{20,16},{24,20},{28,24},{0,28},{5,1},{9... | collective-permute-start | bytes 4718600 | tf_op jit(solution)/shard_map/ppermute | solution.py:39
  118.3 41.1 %collective-permute-start.3 = (s32[192]{0:T(256)S(1)}, s32[192]{0:T(256)S(1)}, u32[]{:S(2)}, u32[]{:S(2)}) collective-permute-start(s32[192]{0:T(256)S(1)} %collective-permute-done.2), channel_id=1, source_target_pairs={{4,0},{8,4},{12,8},{16,12},{20,16},{24,20},{28,24},{0,28},{5,1},{9... | collective-permute-start | bytes 2312 | tf_op jit(solution)/shard_map/ppermute | solution.py:39
  119.3 41.7 %collective-permute-start.1 = (s32[192]{0:T(256)S(1)}, s32[192]{0:T(256)S(1)}, u32[]{:S(2)}, u32[]{:S(2)}) collective-permute-start(s32[192]{0:T(256)S(1)} %collective-permute-done), channel_id=1, source_target_pairs={{28,0},{0,4},{4,8},{8,12},{12,16},{16,20},{20,24},{24,28},{29,1},{... | collective-permute-start | bytes 2312 | tf_op jit(solution)/shard_map/ppermute | solution.py:39
  179.9 11.0 %copy-start = (bf16[192,64,64]{2,1,0:T(8,128)(2,1)S(1)}, bf16[192,64,64]{2,1,0:T(8,128)(2,1)}, u32[]{:S(2)}) copy-start(bf16[192,64,64]{2,1,0:T(8,128)(2,1)} %copy.44) | copy-start | bytes 4718596
Sparse Core Ops, SparseCore 0:
  286.9 54.6 reduce-scatter.1
